TPU v7x, 512 devices: a whole 4x8x8 slice. The times are simulated.
512 devices in a mesh: section: 8 (over y), dp: 64 (over x, z, core).
Axes of the slice: x: 4, y: 8, z: 8, core: 2. Of those that a mesh axis runs over, the one named last changes fastest.
Arguments:
- queries: bfloat16 [65536, 3584], P(('section', 'dp')), may hold values from -1 to 1
- passages: bfloat16 [128, 64, 3584], P('dp'), may hold values from -1 to 1
- candidates: int32 [512, 3], P('section'), may hold values from 0 to 63, as said below
- counts: int32 [512], P('section'), may hold values from 1 to 3, 1024 in all
- teacher: float32 [65536, 384], P(('section', 'dp')), may hold values from -20 to 450
- section_weights: bfloat16 [8, 3584, 3584], P('section', 'dp'), may hold values from -0.09375 to 0.09375
- section_inputs: bfloat16 [8, 64, 3584], P('section', None, 'dp'), may hold values from -1.5 to 1.5
- pre_acts: bfloat16 [8, 64, 3584], P('section', None, 'dp'), may hold values from -8 to 8
Outputs:
- query_grads: bfloat16 [65536, 3584], P(('section', 'dp'))
- passage_grads: bfloat16 [128, 64, 3584], P('dp')
- grad_inputs: float32 [8, 64, 3584], P('section', None, 'dp')
- weight_grads: bfloat16 [8, 3584, 3584], P('section', 'dp')
Inputs may be any that keep to these rules, and one draw needn't show every extreme that they name: `candidates`: each row names 3 different passage blocks. A query block uses the first counts[b] entries of its row of candidates.
All inputs are finite; a program needn't handle non-finite values.
Results may differ from a plain program's by a relative error of at most 0.0085.
Values may be sent and summed in bfloat16 or wider, within the bound.
No kernel may reach another device: no remote copies, remote signals or barrier semaphores. Data moves between devices by JAX's collectives and lax.ppermute only.
A program may use at most 64 MiB of HBM per device.

v0:
```python
import jax
import jax.numpy as jnp
from jax import lax
from jax.sharding import PartitionSpec as P

INVERSE_TEMP = 20.0


def passed_along(value, axis, steps):
    count = lax.axis_size(axis)
    initial, last = (max(0, -steps), min(count, count - steps))
    return lax.ppermute(value, axis, [(source, source + steps) for source in range(initial, last)])


def gathered_pieces(value, axis):
    count = lax.axis_size(axis)
    copies = jnp.broadcast_to(value[None], (count,) + value.shape)
    return lax.all_to_all(copies, axis, 0, 0, tiled=True)


def gathered_columns(value, axis):
    count = lax.axis_size(axis)
    copies = jnp.broadcast_to(value[None], (count,) + value.shape)
    pieces = lax.all_to_all(copies, axis, 0, 0, tiled=True)
    return jnp.transpose(pieces, (1, 0, 2)).reshape(value.shape[0], count * value.shape[1])


def soft_weights(logits, valid):
    masked = jnp.where(valid, logits, -1e30)
    highest = jnp.max(masked, axis=-1, keepdims=True)
    expons = jnp.where(valid, jnp.exp(masked - highest), 0.0)
    return expons / jnp.sum(expons, axis=-1, keepdims=True)


def body(queries, passages, candidates, counts, teacher, section_weights, section_inputs, pre_acts):
    dp_count = lax.axis_size("dp")
    dp_index = lax.axis_index("dp")
    stripe, block_total, width = passages.shape
    row_block_count = stripe * dp_count
    blocks_here = candidates.shape[0] // dp_count
    slot_count = candidates.shape[1]
    requests = blocks_here * slot_count
    all_slots = candidates.reshape(-1)
    chooser = (all_slots[:, None] == jnp.arange(block_total, dtype=jnp.int32)[None, :]).astype(
        passages.dtype
    )
    outgoing = jnp.einsum(
        "rpj,sp->rsj", passages, chooser, preferred_element_type=jnp.float32
    ).astype(passages.dtype)
    pulled_rows = lax.all_to_all(outgoing, "dp", split_axis=1, concat_axis=0, tiled=True)
    pulled_rows = pulled_rows.reshape(row_block_count, blocks_here, slot_count, width)
    own_counts = lax.dynamic_slice_in_dim(counts, dp_index * blocks_here, blocks_here)
    slot_valid = jnp.arange(slot_count, dtype=jnp.int32)[None, :] < own_counts[:, None]
    column_valid = jnp.repeat(slot_valid, row_block_count, axis=1)[:, None, :]
    query_row_items = queries.reshape(blocks_here, row_block_count, width)
    logits = (
        jnp.einsum(
            "ixp,wifp->ixfw", query_row_items, pulled_rows, preferred_element_type=jnp.float32
        )
        * INVERSE_TEMP
    )
    logits = logits.reshape(blocks_here, row_block_count, slot_count * row_block_count)
    target_logits = soft_weights(
        teacher.reshape(blocks_here, row_block_count, slot_count * row_block_count), column_valid
    )
    weight_matrices = (soft_weights(logits, column_valid) - target_logits).astype(jnp.bfloat16)
    weight_matrices = weight_matrices.reshape(
        blocks_here, row_block_count, slot_count, row_block_count
    )
    query_sums = (
        jnp.einsum(
            "geal,lgay->gey", weight_matrices, pulled_rows, preferred_element_type=jnp.float32
        )
        * INVERSE_TEMP
    )
    passage_sums = (
        jnp.einsum(
            "fnyw,fnj->wfyj", weight_matrices, query_row_items, preferred_element_type=jnp.float32
        )
        * INVERSE_TEMP
    )
    block_terms = passage_sums.reshape(row_block_count, requests, width).astype(jnp.bfloat16)
    micro_count = section_inputs.shape[1] // dp_count
    col_width = width // dp_count
    micro_cols = jnp.transpose(
        query_sums[0, :micro_count].reshape(micro_count, dp_count, col_width), (1, 0, 2)
    )
    section_count = lax.axis_size("section")
    chunk = width // section_count
    term_pieces = passage_sums.reshape(dp_count, stripe, requests, section_count, chunk)
    term_pieces = jnp.transpose(term_pieces, (3, 0, 1, 2, 4)).astype(jnp.bfloat16)
    term_pieces = term_pieces.reshape(section_count * dp_count, stripe, requests, chunk)
    own_slots = lax.dynamic_slice_in_dim(all_slots, dp_index * requests, requests)
    slot_tags = jnp.broadcast_to(
        own_slots.astype(jnp.bfloat16)[None, None, :, None],
        (section_count * dp_count, stripe, requests, 1),
    )
    term_pieces = jnp.concatenate([term_pieces, slot_tags], axis=3)
    incoming_terms = lax.all_to_all(
        term_pieces, ("section", "dp"), split_axis=0, concat_axis=0, tiled=True
    )
    last_section = section_count - 1
    packed = jnp.concatenate(
        [section_weights[0].reshape(col_width, dp_count, col_width), pre_acts[0][None]]
    )
    moved = tuple(
        (
            lax.ppermute(packed, "section", [(source, last_section)])
            for source in range(last_section)
        )
    )
    incoming_terms, carry_start, moved = lax.optimization_barrier(
        (incoming_terms, micro_cols, moved)
    )
    packed_of = dict(enumerate(moved))
    packed_of[last_section] = packed
    every_slot = incoming_terms[:, 0, :, chunk].astype(jnp.int32)
    onehot = (every_slot[:, :, None] == jnp.arange(block_total, dtype=jnp.int32)).astype(
        jnp.bfloat16
    )
    dense = jnp.einsum(
        "qsfc,qfn->snc", incoming_terms[:, :, :, :chunk], onehot, preferred_element_type=jnp.float32
    )
    dense = dense.reshape(stripe, block_total, chunk).astype(jnp.bfloat16)
    passage_out = gathered_columns(dense.reshape(stripe * block_total, chunk), "section")
    passage_out = passage_out.reshape(stripe, block_total, width)
    entry = lax.all_to_all(carry_start, "dp", split_axis=0, concat_axis=1, tiled=True)
    section_index = lax.axis_index("section")
    last = section_count - 1
    carry = entry.reshape(dp_count * micro_count, col_width)
    sent_of = {}
    for source in range(last, -1, -1):
        rows = packed_of[source][:col_width]
        pre = packed_of[source][col_width].astype(jnp.float32)
        sigma = jax.nn.sigmoid(pre)
        slope = sigma * (1.0 + pre * (1.0 - sigma))
        inner = (carry * slope).astype(jnp.bfloat16)
        piece = gathered_pieces(inner, "dp")
        back_sum = jnp.einsum("dmj,idj->mi", piece, rows, preferred_element_type=jnp.float32)
        carry = carry + back_sum
        if source == last:
            grad_cols, home_inner = (carry, inner)
        else:
            both = jnp.stack([carry, inner.astype(jnp.float32)])
            sent_of[source] = lax.ppermute(both, "section", [(last, source)])
    for source in range(last):
        here = section_index == source
        grad_cols = jnp.where(here, sent_of[source][0], grad_cols)
        home_inner = jnp.where(here, sent_of[source][1].astype(jnp.bfloat16), home_inner)
    home_piece = gathered_pieces(home_inner, "dp")
    grad_weight = (
        jnp.einsum("mi,dmj->idj", section_inputs[0], home_piece, preferred_element_type=jnp.float32)
        .reshape(col_width, width)
        .astype(jnp.bfloat16)
    )
    return (
        query_sums.reshape(blocks_here * row_block_count, width).astype(jnp.bfloat16),
        passage_out,
        grad_cols[None],
        grad_weight[None],
    )


def solution(mesh):
    placed = (
        P(("section", "dp"), None),
        P("dp", None, None),
        P("section", None),
        P("section"),
        P(("section", "dp"), None),
        P("section", "dp", None),
        P("section", None, "dp"),
        P("section", None, "dp"),
    )
    return jax.shard_map(
        body,
        mesh=mesh,
        in_specs=placed,
        out_specs=(
            P(("section", "dp"), None),
            P("dp", None, None),
            P("section", None, "dp"),
            P("section", "dp", None),
        ),
        check_vma=False,
    )
```

profile of v0, /device:TPU:1, one launch (start us, length us, event | category | flops | bytes accessed | tf_op | source)
XLA Modules:
  0.0 601.3 jit_solution(9847557009770879357)
XLA Ops:
  3.7 4.4 copy.128
  8.1 15.1 %all-to-all-start = ((bf16[2,192,3584]{2,0,1:T(2,128)(2,1)}), bf16[2,192,3584]{2,0,1:T(2,128)(2,1)}, u32[]{:S(2)}, u32[]{:S(2)}) async-start(bf16[2,192,3584]{2,0,1:T(2,128)(2,1)} %copy.128), calls=%async_computation | async-start | bytes 5505024 | tf_op jit(solution)/shard_map/all_to_all | solution.py:50
  25.1 63.2 %all-to-all-done = bf16[2,192,3584]{2,0,1:T(2,128)(2,1)} async-done(((bf16[2,192,3584]{2,0,1:T(2,128)(2,1)}), bf16[2,192,3584]{2,0,1:T(2,128)(2,1)}, u32[]{:S(2)}, u32[]{:S(2)}) %all-to-all-start) | async-done | bytes 2752544 | tf_op jit(solution)/shard_map/all_to_all | solution.py:50
  88.3 5.2 copy.129
  93.5 6.8 %reshape.247 = bf16[128,3,3584]{2,0,1:T(8,128)(2,1)} reshape(bf16[64,2,3,3584]{3,1,0,2:T(2,128)(2,1)} %copy.129) | data formatting | bytes 5505024 | tf_op jit(solution)/shard_map/reshape.5
  105.7 6.8 %convert_element_type.163 = bf16[64,2,3,8,448]{4,3,1,0,2:T(8,128)(2,1)} reshape(bf16[128,1,3,3584]{3,0,2,1:T(8,128)(2,1)} %fusion.2) | data formatting | bytes 5505024 | tf_op jit(solution)/shard_map/convert_element_type | solution.py:91
  112.4 3.6 copy.132
  116.8 4.9 copy.133
  121.7 14.9 %all-to-all-start.1 = ((bf16[512,2,3,449]{3,1,2,0:T(2,128)(2,1)}), bf16[512,2,3,449]{3,1,2,0:T(2,128)(2,1)}, u32[]{:S(2)}, u32[]{:S(2)}) async-start(bf16[512,2,3,449]{3,1,2,0:T(2,128)(2,1)} %copy.133), calls=%async_computation.1 | async-start | bytes 6291456 | tf_op jit(solution)/shard_map/all_to_all | solution.py:99
  139.3 4.9 collective-permute-start
  149.6 117.1 %collective-permute-done = bf16[57,64,56]{1,2,0:T(8,128)(2,1)S(1)} collective-permute-done((bf16[57,64,56]{1,2,0:T(8,128)(2,1)S(1)}, bf16[57,64,56]{1,2,0:T(8,128)(2,1)S(1)}, u32[]{:S(2)}, u32[]{:S(2)}) %collective-permute-start) | collective-permute-done | bytes 408608 | tf_op jit(solution)/shard_map/ppermute | solution.py:108
  274.2 23.9 %all_to_all.79 = f32[64,1,56]{2,1,0:T(1,128)S(1)} all-to-all(f32[64,1,56]{2,1,0:T(1,128)S(1)} %bitcast.302), channel_id=1, replica_groups=mesh['section'=8,'dp'=64] {'dp'}, dimensions={0} | all-to-all | bytes 28672 | tf_op jit(solution)/shard_map/all_to_all | solution.py:127
  299.6 19.9 %all_to_all.80 = bf16[64,2,1792]{2,1,0:T(2,128)(2,1)S(1)} all-to-all(bf16[64,2,1792]{2,1,0:T(2,128)(2,1)S(1)} %reshape.284), channel_id=1, replica_groups=mesh['section'=8,'dp'=64] {'dp'}, dimensions={0} | all-to-all | bytes 917504 | tf_op jit(solution)/shard_map/all_to_all | solution.py:18
  323.7 6.3 %all-to-all-start.5 = ((bf16[64,2,1792]{2,1,0:T(2,128)(2,1)}), bf16[64,2,1792]{2,1,0:T(2,128)(2,1)S(1)}, u32[]{:S(2)}, u32[]{:S(2)}) async-start(bf16[64,2,1792]{2,1,0:T(2,128)(2,1)} %reshape.286), calls=%async_computation.5 | async-start | bytes 917504 | tf_op jit(solution)/shard_map/all_to_all | solution.py:18
  333.4 12.5 %all-to-all-done.5 = bf16[64,2,1792]{2,1,0:T(2,128)(2,1)S(1)} async-done(((bf16[64,2,1792]{2,1,0:T(2,128)(2,1)}), bf16[64,2,1792]{2,1,0:T(2,128)(2,1)S(1)}, u32[]{:S(2)}, u32[]{:S(2)}) %all-to-all-start.5) | async-done | bytes 458784 | tf_op jit(solution)/shard_map/all_to_all | solution.py:18
  349.7 6.3 %all-to-all-start.6 = ((bf16[64,2,1792]{2,1,0:T(2,128)(2,1)}), bf16[64,2,1792]{2,1,0:T(2,128)(2,1)S(1)}, u32[]{:S(2)}, u32[]{:S(2)}) async-start(bf16[64,2,1792]{2,1,0:T(2,128)(2,1)} %reshape.288), calls=%async_computation.6 | async-start | bytes 917504 | tf_op jit(solution)/shard_map/all_to_all | solution.py:18
  359.4 12.5 %all-to-all-done.6 = bf16[64,2,1792]{2,1,0:T(2,128)(2,1)S(1)} async-done(((bf16[64,2,1792]{2,1,0:T(2,128)(2,1)}), bf16[64,2,1792]{2,1,0:T(2,128)(2,1)S(1)}, u32[]{:S(2)}, u32[]{:S(2)}) %all-to-all-start.6) | async-done | bytes 458784 | tf_op jit(solution)/shard_map/all_to_all | solution.py:18
  375.7 6.3 %all-to-all-start.7 = ((bf16[64,2,1792]{2,1,0:T(2,128)(2,1)}), bf16[64,2,1792]{2,1,0:T(2,128)(2,1)S(1)}, u32[]{:S(2)}, u32[]{:S(2)}) async-start(bf16[64,2,1792]{2,1,0:T(2,128)(2,1)} %reshape.290), calls=%async_computation.7 | async-start | bytes 917504 | tf_op jit(solution)/shard_map/all_to_all | solution.py:18
  385.4 12.5 %all-to-all-done.7 = bf16[64,2,1792]{2,1,0:T(2,128)(2,1)S(1)} async-done(((bf16[64,2,1792]{2,1,0:T(2,128)(2,1)}), bf16[64,2,1792]{2,1,0:T(2,128)(2,1)S(1)}, u32[]{:S(2)}, u32[]{:S(2)}) %all-to-all-start.7) | async-done | bytes 458784 | tf_op jit(solution)/shard_map/all_to_all | solution.py:18
  401.7 6.3 %all-to-all-start.8 = ((bf16[64,2,1792]{2,1,0:T(2,128)(2,1)}), bf16[64,2,1792]{2,1,0:T(2,128)(2,1)S(1)}, u32[]{:S(2)}, u32[]{:S(2)}) async-start(bf16[64,2,1792]{2,1,0:T(2,128)(2,1)} %reshape.292), calls=%async_computation.8 | async-start | bytes 917504 | tf_op jit(solution)/shard_map/all_to_all | solution.py:18
  411.4 12.5 %all-to-all-done.8 = bf16[64,2,1792]{2,1,0:T(2,128)(2,1)S(1)} async-done(((bf16[64,2,1792]{2,1,0:T(2,128)(2,1)}), bf16[64,2,1792]{2,1,0:T(2,128)(2,1)S(1)}, u32[]{:S(2)}, u32[]{:S(2)}) %all-to-all-start.8) | async-done | bytes 458784 | tf_op jit(solution)/shard_map/all_to_all | solution.py:18
  427.6 6.3 %all-to-all-start.9 = ((bf16[64,2,1792]{2,1,0:T(2,128)(2,1)}), bf16[64,2,1792]{2,1,0:T(2,128)(2,1)S(1)}, u32[]{:S(2)}, u32[]{:S(2)}) async-start(bf16[64,2,1792]{2,1,0:T(2,128)(2,1)} %reshape.294), calls=%async_computation.9 | async-start | bytes 917504 | tf_op jit(solution)/shard_map/all_to_all | solution.py:18
  437.3 12.5 %all-to-all-done.9 = bf16[64,2,1792]{2,1,0:T(2,128)(2,1)S(1)} async-done(((bf16[64,2,1792]{2,1,0:T(2,128)(2,1)}), bf16[64,2,1792]{2,1,0:T(2,128)(2,1)S(1)}, u32[]{:S(2)}, u32[]{:S(2)}) %all-to-all-start.9) | async-done | bytes 458784 | tf_op jit(solution)/shard_map/all_to_all | solution.py:18
  453.6 6.6 %all-to-all-start.10 = ((bf16[64,2,1792]{2,1,0:T(2,128)(2,1)}), bf16[64,2,1792]{2,1,0:T(2,128)(2,1)S(1)}, u32[]{:S(2)}, u32[]{:S(2)}) async-start(bf16[64,2,1792]{2,1,0:T(2,128)(2,1)} %reshape.296), calls=%async_computation.10 | async-start | bytes 917504 | tf_op jit(solution)/shard_map/all_to_all | solution.py:18
  463.6 12.4 %all-to-all-done.10 = bf16[64,2,1792]{2,1,0:T(2,128)(2,1)S(1)} async-done(((bf16[64,2,1792]{2,1,0:T(2,128)(2,1)}), bf16[64,2,1792]{2,1,0:T(2,128)(2,1)S(1)}, u32[]{:S(2)}, u32[]{:S(2)}) %all-to-all-start.10) | async-done | bytes 458784 | tf_op jit(solution)/shard_map/all_to_all | solution.py:18
  479.0 6.3 %all-to-all-start.11 = ((bf16[64,2,1792]{2,1,0:T(2,128)(2,1)}), bf16[64,2,1792]{2,1,0:T(2,128)(2,1)S(1)}, u32[]{:S(2)}, u32[]{:S(2)}) async-start(bf16[64,2,1792]{2,1,0:T(2,128)(2,1)} %reshape.298), calls=%async_computation.11 | async-start | bytes 917504 | tf_op jit(solution)/shard_map/all_to_all | solution.py:18
  485.3 8.7 %copy.135 = bf16[512,2,3,449]{0,3,2,1:T(8,128)(2,1)} copy(bf16[512,2,3,449]{3,1,2,0:T(2,128)(2,1)} %all-to-all-done.1) | data formatting | bytes 5517312 | tf_op jit(solution)/shard_map/optimization_barrier | solution.py:112
  497.6 3.6 all-to-all-done.11
  502.4 37.4 %all-to-all-start.2 = ((bf16[8,128,448]{1,2,0:T(8,128)(2,1)}), bf16[8,128,448]{1,2,0:T(8,128)(2,1)S(1)}, u32[]{:S(2)}, u32[]{:S(2)}) async-start(bf16[8,128,448]{1,2,0:T(8,128)(2,1)} %broadcast_in_dim.137), calls=%async_computation.2 | async-start | bytes 1835008 | tf_op jit(solution)/shard_map/all_to_all | solution.py:24
  553.5 13.6 %collective-permute-done.13 = f32[2,64,56]{1,2,0:T(8,128)S(1)} collective-permute-done((f32[2,64,56]{1,2,0:T(8,128)S(1)}, f32[2,64,56]{1,2,0:T(8,128)S(1)}, u32[]{:S(2)}, u32[]{:S(2)}) %collective-permute-start.13) | collective-permute-done | bytes 28704 | tf_op jit(solution)/shard_map/ppermute | solution.py:145
  569.3 10.5 %all-to-all-start.12 = ((bf16[64,2,1792]{2,1,0:T(2,128)(2,1)}), bf16[64,2,1792]{2,1,0:T(2,128)(2,1)S(1)}, u32[]{:S(2)}, u32[]{:S(2)}) async-start(bf16[64,2,1792]{2,1,0:T(2,128)(2,1)} %reshape.300), calls=%async_computation.12 | async-start | bytes 917504 | tf_op jit(solution)/shard_map/all_to_all | solution.py:18
  584.5 11.1 %all-to-all-done.12 = bf16[64,2,1792]{2,1,0:T(2,128)(2,1)S(1)} async-done(((bf16[64,2,1792]{2,1,0:T(2,128)(2,1)}), bf16[64,2,1792]{2,1,0:T(2,128)(2,1)S(1)}, u32[]{:S(2)}, u32[]{:S(2)}) %all-to-all-start.12) | async-done | bytes 458784 | tf_op jit(solution)/shard_map/all_to_all | solution.py:18
  (173 shorter events, 104.8 us)
Async XLA Ops:
  0.6 99.6 %copy-start = (bf16[128,3584]{1,0:T(8,128)(2,1)S(1)}, bf16[128,3584]{1,0:T(8,128)(2,1)}, u32[]{:S(2)}) copy-start(bf16[128,3584]{1,0:T(8,128)(2,1)} %param.8) | copy-start | bytes 2752516
  8.1 80.2 %all-to-all-start = ((bf16[2,192,3584]{2,0,1:T(2,128)(2,1)}), bf16[2,192,3584]{2,0,1:T(2,128)(2,1)}, u32[]{:S(2)}, u32[]{:S(2)}) async-start(bf16[2,192,3584]{2,0,1:T(2,128)(2,1)} %copy.128), calls=%async_computation | async-start | bytes 5505024 | tf_op jit(solution)/shard_map/all_to_all | solution.py:50
  121.7 152.5 %all-to-all-start.1 = ((bf16[512,2,3,449]{3,1,2,0:T(2,128)(2,1)}), bf16[512,2,3,449]{3,1,2,0:T(2,128)(2,1)}, u32[]{:S(2)}, u32[]{:S(2)}) async-start(bf16[512,2,3,449]{3,1,2,0:T(2,128)(2,1)} %copy.133), calls=%async_computation.1 | async-start | bytes 6291456 | tf_op jit(solution)/shard_map/all_to_all | solution.py:99
  139.3 127.4 %collective-permute-start = (bf16[57,64,56]{1,2,0:T(8,128)(2,1)S(1)}, bf16[57,64,56]{1,2,0:T(8,128)(2,1)S(1)}, u32[]{:S(2)}, u32[]{:S(2)}) collective-permute-start(bf16[57,64,56]{1,2,0:T(8,128)(2,1)S(1)} %pad_maximum_fusion.1), channel_id=1, source_target_pairs={{0,448},{1,449},{2,450},{3,451},{4,452},{5,453},{6,454},{7,455},{8... | collective-permute-start | bytes 1225736 | tf_op jit(solution)/shard_map/ppermute | solution.py:108
  144.2 124.1 %collective-permute-start.1 = (bf16[57,64,56]{1,2,0:T(8,128)(2,1)S(1)}, bf16[57,64,56]{1,2,0:T(8,128)(2,1)S(1)}, u32[]{:S(2)}, u32[]{:S(2)}) collective-permute-start(bf16[57,64,56]{1,2,0:T(8,128)(2,1)S(1)} %pad_maximum_fusion.1), channel_id=1, source_target_pairs={{64,448},{65,449},{66,450},{67,451},{68,452},{69,453},{70,454},{71... | collective-permute-start | bytes 1225736 | tf_op jit(solution)/shard_map/ppermute | solution.py:108
  144.9 129.3 %collective-permute-start.2 = (bf16[57,64,56]{1,2,0:T(8,128)(2,1)S(1)}, bf16[57,64,56]{1,2,0:T(8,128)(2,1)}, u32[]{:S(2)}, u32[]{:S(2)}) collective-permute-start(bf16[57,64,56]{1,2,0:T(8,128)(2,1)S(1)} %pad_maximum_fusion.1), channel_id=1, source_target_pairs={{128,448},{129,449},{130,450},{131,451},{132,452},{133,453},{134,4... | collective-permute-start | bytes 1225736 | tf_op jit(solution)/shard_map/ppermute | solution.py:108
  146.5 127.7 %collective-permute-start.3 = (bf16[57,64,56]{1,2,0:T(8,128)(2,1)S(1)}, bf16[57,64,56]{1,2,0:T(8,128)(2,1)}, u32[]{:S(2)}, u32[]{:S(2)}) collective-permute-start(bf16[57,64,56]{1,2,0:T(8,128)(2,1)S(1)} %pad_maximum_fusion.1), channel_id=1, source_target_pairs={{192,448},{193,449},{194,450},{195,451},{196,452},{197,453},{198,4... | collective-permute-start | bytes 1225736 | tf_op jit(solution)/shard_map/ppermute | solution.py:108
  148.0 126.2 %collective-permute-start.4 = (bf16[57,64,56]{1,2,0:T(8,128)(2,1)S(1)}, bf16[57,64,56]{1,2,0:T(8,128)(2,1)}, u32[]{:S(2)}, u32[]{:S(2)}) collective-permute-start(bf16[57,64,56]{1,2,0:T(8,128)(2,1)S(1)} %pad_maximum_fusion.1), channel_id=1, source_target_pairs={{256,448},{257,449},{258,450},{259,451},{260,452},{261,453},{262,4... | collective-permute-start | bytes 1225736 | tf_op jit(solution)/shard_map/ppermute | solution.py:108
  266.7 209.8 %copy-start.2 = (bf16[57,64,56]{1,2,0:T(8,128)(2,1)}, bf16[57,64,56]{1,2,0:T(8,128)(2,1)S(1)}, u32[]{:S(2)}) copy-start(bf16[57,64,56]{1,2,0:T(8,128)(2,1)S(1)} %collective-permute-done) | copy-start | bytes 1225732
  266.7 7.5 %collective-permute-start.5 = (bf16[57,64,56]{1,2,0:T(8,128)(2,1)S(1)}, bf16[57,64,56]{1,2,0:T(8,128)(2,1)}, u32[]{:S(2)}, u32[]{:S(2)}) collective-permute-start(bf16[57,64,56]{1,2,0:T(8,128)(2,1)S(1)} %pad_maximum_fusion.1), channel_id=1, source_target_pairs={{320,448},{321,449},{322,450},{323,451},{324,452},{325,453},{326,4... | collective-permute-start | bytes 1225736 | tf_op jit(solution)/shard_map/ppermute | solution.py:108
  269.2 5.1 collective-permute-start.6
  323.7 22.3 %all-to-all-start.5 = ((bf16[64,2,1792]{2,1,0:T(2,128)(2,1)}), bf16[64,2,1792]{2,1,0:T(2,128)(2,1)S(1)}, u32[]{:S(2)}, u32[]{:S(2)}) async-start(bf16[64,2,1792]{2,1,0:T(2,128)(2,1)} %reshape.286), calls=%async_computation.5 | async-start | bytes 917504 | tf_op jit(solution)/shard_map/all_to_all | solution.py:18
  349.7 22.2 %all-to-all-start.6 = ((bf16[64,2,1792]{2,1,0:T(2,128)(2,1)}), bf16[64,2,1792]{2,1,0:T(2,128)(2,1)S(1)}, u32[]{:S(2)}, u32[]{:S(2)}) async-start(bf16[64,2,1792]{2,1,0:T(2,128)(2,1)} %reshape.288), calls=%async_computation.6 | async-start | bytes 917504 | tf_op jit(solution)/shard_map/all_to_all | solution.py:18
  375.7 22.2 %all-to-all-start.7 = ((bf16[64,2,1792]{2,1,0:T(2,128)(2,1)}), bf16[64,2,1792]{2,1,0:T(2,128)(2,1)S(1)}, u32[]{:S(2)}, u32[]{:S(2)}) async-start(bf16[64,2,1792]{2,1,0:T(2,128)(2,1)} %reshape.290), calls=%async_computation.7 | async-start | bytes 917504 | tf_op jit(solution)/shard_map/all_to_all | solution.py:18
  401.7 22.2 %all-to-all-start.8 = ((bf16[64,2,1792]{2,1,0:T(2,128)(2,1)}), bf16[64,2,1792]{2,1,0:T(2,128)(2,1)S(1)}, u32[]{:S(2)}, u32[]{:S(2)}) async-start(bf16[64,2,1792]{2,1,0:T(2,128)(2,1)} %reshape.292), calls=%async_computation.8 | async-start | bytes 917504 | tf_op jit(solution)/shard_map/all_to_all | solution.py:18
  427.6 22.2 %all-to-all-start.9 = ((bf16[64,2,1792]{2,1,0:T(2,128)(2,1)}), bf16[64,2,1792]{2,1,0:T(2,128)(2,1)S(1)}, u32[]{:S(2)}, u32[]{:S(2)}) async-start(bf16[64,2,1792]{2,1,0:T(2,128)(2,1)} %reshape.294), calls=%async_computation.9 | async-start | bytes 917504 | tf_op jit(solution)/shard_map/all_to_all | solution.py:18
  453.6 22.4 %all-to-all-start.10 = ((bf16[64,2,1792]{2,1,0:T(2,128)(2,1)}), bf16[64,2,1792]{2,1,0:T(2,128)(2,1)S(1)}, u32[]{:S(2)}, u32[]{:S(2)}) async-start(bf16[64,2,1792]{2,1,0:T(2,128)(2,1)} %reshape.296), calls=%async_computation.10 | async-start | bytes 917504 | tf_op jit(solution)/shard_map/all_to_all | solution.py:18
  479.0 22.2 %all-to-all-start.11 = ((bf16[64,2,1792]{2,1,0:T(2,128)(2,1)}), bf16[64,2,1792]{2,1,0:T(2,128)(2,1)S(1)}, u32[]{:S(2)}, u32[]{:S(2)}) async-start(bf16[64,2,1792]{2,1,0:T(2,128)(2,1)} %reshape.298), calls=%async_computation.11 | async-start | bytes 917504 | tf_op jit(solution)/shard_map/all_to_all | solution.py:18
  494.8 45.0 %copy-start.3 = (bf16[57,64,56]{1,2,0:T(8,128)(2,1)S(1)}, bf16[57,64,56]{1,2,0:T(8,128)(2,1)}, u32[]{:S(2)}) copy-start(bf16[57,64,56]{1,2,0:T(8,128)(2,1)} %copy-done.2) | copy-start | bytes 1225732
  502.3 46.1 %copy-start.9 = (f32[64,56]{0,1:T(8,128)S(1)}, f32[64,56]{0,1:T(8,128)}, u32[]{:S(2)}) copy-start(f32[64,56]{0,1:T(8,128)} %copy-done.8) | copy-start | bytes 43012
  502.3 46.1 %copy-start.17 = (f32[1,64,56]{1,2,0:T(8,128)S(1)}, f32[1,64,56]{1,2,0:T(8,128)}, u32[]{:S(2)}) copy-start(f32[1,64,56]{1,2,0:T(8,128)} %get-tuple-element.30) | copy-start | bytes 43012
  502.3 47.4 %copy-start.10 = (f32[64,56]{0,1:T(8,128)S(1)}, f32[64,56]{0,1:T(8,128)}, u32[]{:S(2)}) copy-start(f32[64,56]{0,1:T(8,128)} %get-tuple-element.46) | copy-start | bytes 43012
  502.3 47.4 %copy-start.18 = (f32[1,64,56]{1,2,0:T(8,128)S(1)}, f32[1,64,56]{1,2,0:T(8,128)}, u32[]{:S(2)}) copy-start(f32[1,64,56]{1,2,0:T(8,128)} %get-tuple-element.32) | copy-start | bytes 43012
  502.4 67.0 %all-to-all-start.2 = ((bf16[8,128,448]{1,2,0:T(8,128)(2,1)}), bf16[8,128,448]{1,2,0:T(8,128)(2,1)S(1)}, u32[]{:S(2)}, u32[]{:S(2)}) async-start(bf16[8,128,448]{1,2,0:T(8,128)(2,1)} %broadcast_in_dim.137), calls=%async_computation.2 | async-start | bytes 1835008 | tf_op jit(solution)/shard_map/all_to_all | solution.py:24
  542.7 8.7 %collective-permute-start.7 = (f32[2,64,56]{1,2,0:T(8,128)}, f32[2,64,56]{1,2,0:T(8,128)}, u32[]{:S(2)}, u32[]{:S(2)}) collective-permute-start(f32[2,64,56]{1,2,0:T(8,128)} %pad_maximum_fusion.2), channel_id=1, source_target_pairs={{448,384},{449,385},{450,386},{451,387},{452,388},{453,389},{454,3... | collective-permute-start | bytes 86024 | tf_op jit(solution)/shard_map/ppermute | solution.py:145
  544.6 7.5 %collective-permute-start.8 = (f32[2,64,56]{1,2,0:T(8,128)}, f32[2,64,56]{1,2,0:T(8,128)}, u32[]{:S(2)}, u32[]{:S(2)}) collective-permute-start(f32[2,64,56]{1,2,0:T(8,128)} %pad_maximum_fusion.3), channel_id=1, source_target_pairs={{448,320},{449,321},{450,322},{451,323},{452,324},{453,325},{454,3... | collective-permute-start | bytes 86024 | tf_op jit(solution)/shard_map/ppermute | solution.py:145
  545.9 7.5 %collective-permute-start.9 = (f32[2,64,56]{1,2,0:T(8,128)S(1)}, f32[2,64,56]{1,2,0:T(8,128)}, u32[]{:S(2)}, u32[]{:S(2)}) collective-permute-start(f32[2,64,56]{1,2,0:T(8,128)S(1)} %pad_maximum_fusion.4), channel_id=1, source_target_pairs={{448,256},{449,257},{450,258},{451,259},{452,260},{453,261},{454,2... | collective-permute-start | bytes 86024 | tf_op jit(solution)/shard_map/ppermute | solution.py:145
  547.2 6.3 %collective-permute-start.10 = (f32[2,64,56]{1,2,0:T(8,128)S(1)}, f32[2,64,56]{1,2,0:T(8,128)}, u32[]{:S(2)}, u32[]{:S(2)}) collective-permute-start(f32[2,64,56]{1,2,0:T(8,128)S(1)} %pad_maximum_fusion.5), channel_id=1, source_target_pairs={{448,192},{449,193},{450,194},{451,195},{452,196},{453,197},{454,1... | collective-permute-start | bytes 86024 | tf_op jit(solution)/shard_map/ppermute | solution.py:145
  548.5 5.0 collective-permute-start.11
  551.4 2.0 collective-permute-start.12
  552.1 14.9 %collective-permute-start.13 = (f32[2,64,56]{1,2,0:T(8,128)S(1)}, f32[2,64,56]{1,2,0:T(8,128)S(1)}, u32[]{:S(2)}, u32[]{:S(2)}) collective-permute-start(f32[2,64,56]{1,2,0:T(8,128)S(1)} %pad_maximum_fusion.8), channel_id=1, source_target_pairs={{448,0},{449,1},{450,2},{451,3},{452,4},{453,5},{454,6},{455,7},{4... | collective-permute-start | bytes 86024 | tf_op jit(solution)/shard_map/ppermute | solution.py:145
  569.3 26.3 %all-to-all-start.12 = ((bf16[64,2,1792]{2,1,0:T(2,128)(2,1)}), bf16[64,2,1792]{2,1,0:T(2,128)(2,1)S(1)}, u32[]{:S(2)}, u32[]{:S(2)}) async-start(bf16[64,2,1792]{2,1,0:T(2,128)(2,1)} %reshape.300), calls=%async_computation.12 | async-start | bytes 917504 | tf_op jit(solution)/shard_map/all_to_all | solution.py:18
  (20 other events, 424.6 us)
where the time goes:
time: 612 us; the launch traced here: 601 us
  waiting for transfers between devices  284 us (46%)
  starting transfers between devices  144 us (24%)
  local copies, waits for them, and re-layouts  94.4 us (15%)
  blocking collectives  43.8 us (7%)
  matrix products  26.7 us (4%)
  other arithmetic  7.1 us (1%)
    ppermute x7, waiting for transfers between devices, body(): lax.ppermute(packed, 'section', [(source, last_section)])  117 us
    all_to_all x8, waiting for transfers between devices, gathered_pieces(): return lax.all_to_all(copies, axis, 0, 0, tiled=True)  89.7 us
    all_to_all x1, waiting for transfers between devices, body(): lax.all_to_all(outgoing, 'dp', split_axis=1, concat_axis=0, tiled=True)  63.2 us
    all_to_all x8, starting transfers between devices, gathered_pieces(): return lax.all_to_all(copies, axis, 0, 0, tiled=True)  54.8 us
    all_to_all x1, starting transfers between devices, gathered_columns(): pieces = lax.all_to_all(copies, axis, 0, 0, tiled=True)  37.4 us
    all_to_all x1, blocking collectives, body(): lax.all_to_all(carry_start, 'dp', split_axis=0, concat_axis=1, tiled=True)  23.9 us
    slice x14, local copies, waits for them, and re-layouts, body(): rows = packed_of[source][:col_width]  22.6 us
    all_to_all x1, blocking collectives, gathered_pieces(): return lax.all_to_all(copies, axis, 0, 0, tiled=True)  19.9 us
  transfers between devices with their start and end apart: 25, of which 11 were waited for; matrix products, arithmetic and copies ran while one was open for 9% of the time, Pallas kernels for 0%

commit v1 on v0

--- a/solution.py
+++ b/solution.py
@@ -124,7 +124,10 @@
     dense = dense.reshape(stripe, block_total, chunk).astype(jnp.bfloat16)
     passage_out = gathered_columns(dense.reshape(stripe * block_total, chunk), "section")
     passage_out = passage_out.reshape(stripe, block_total, width)
-    entry = lax.all_to_all(carry_start, "dp", split_axis=0, concat_axis=1, tiled=True)
+    d_next = jax.lax.all_to_all(
+        jnp.stack(jnp.split(carry_start, jax.lax.axis_size("dp"), axis=0)), "dp", 0, 0
+    )
+    entry = jnp.concatenate(d_next, axis=1)
     section_index = lax.axis_index("section")
     last = section_count - 1
     carry = entry.reshape(dp_count * micro_count, col_width)

time: 612 us -> 613 us (level)
    unnamed x84 -> x147, local copies, waits for them, and re-layouts: 19.7 us -> 20.3 us
where the time goes in v1:
time: 613 us; the launch traced here: 602 us
  waiting for transfers between devices  284 us (46%)
  starting transfers between devices  144 us (23%)
  local copies, waits for them, and re-layouts  95.1 us (16%)
  blocking collectives  43.6 us (7%)
  matrix products  26.7 us (4%)
  other arithmetic  7.1 us (1%)
    ppermute x7, waiting for transfers between devices, body(): lax.ppermute(packed, 'section', [(source, last_section)])  117 us
    all_to_all x8, waiting for transfers between devices, gathered_pieces(): return lax.all_to_all(copies, axis, 0, 0, tiled=True)  89.7 us
    all_to_all x1, waiting for transfers between devices, body(): lax.all_to_all(outgoing, 'dp', split_axis=1, concat_axis=0, tiled=True)  63.2 us
    all_to_all x8, starting transfers between devices, gathered_pieces(): return lax.all_to_all(copies, axis, 0, 0, tiled=True)  54.8 us
    all_to_all x1, starting transfers between devices, gathered_columns(): pieces = lax.all_to_all(copies, axis, 0, 0, tiled=True)  37 us
    all_to_all x1, blocking collectives, body(): jax.lax.all_to_all(jnp.stack(jnp.split(carry_start, jax.lax.axis_size('dp...  23.7 us
    slice x14, local copies, waits for them, and re-layouts, body(): rows = packed_of[source][:col_width]  22.6 us
    unnamed x147, local copies, waits for them, and re-layouts  20.3 us
  transfers between devices with their start and end apart: 25, of which 11 were waited for; matrix products, arithmetic and copies ran while one was open for 9% of the time, Pallas kernels for 0%

profile of v1, /device:TPU:1, one launch (start us, length us, event | category | flops | bytes accessed | tf_op | source)
XLA Modules:
  0.0 602.1 jit_solution(5663581825155474104)
XLA Ops:
  3.7 4.4 copy.315
  8.1 15.1 %all-to-all-start = ((bf16[2,192,3584]{2,0,1:T(2,128)(2,1)}), bf16[2,192,3584]{2,0,1:T(2,128)(2,1)}, u32[]{:S(2)}, u32[]{:S(2)}) async-start(bf16[2,192,3584]{2,0,1:T(2,128)(2,1)} %copy.315), calls=%async_computation | async-start | bytes 5505024 | tf_op jit(solution)/shard_map/all_to_all | solution.py:50
  25.1 63.2 %all-to-all-done = bf16[2,192,3584]{2,0,1:T(2,128)(2,1)} async-done(((bf16[2,192,3584]{2,0,1:T(2,128)(2,1)}), bf16[2,192,3584]{2,0,1:T(2,128)(2,1)}, u32[]{:S(2)}, u32[]{:S(2)}) %all-to-all-start) | async-done | bytes 2752544 | tf_op jit(solution)/shard_map/all_to_all | solution.py:50
  88.3 5.2 copy.316
  93.5 6.8 %reshape.238 = bf16[128,3,3584]{2,0,1:T(8,128)(2,1)} reshape(bf16[64,2,3,3584]{3,1,0,2:T(2,128)(2,1)} %copy.316) | data formatting | bytes 5505024 | tf_op jit(solution)/shard_map/reshape.5
  105.7 6.8 %convert_element_type.163 = bf16[64,2,3,8,448]{4,3,1,0,2:T(8,128)(2,1)} reshape(bf16[128,1,3,3584]{3,0,2,1:T(8,128)(2,1)} %fusion.2) | data formatting | bytes 5505024 | tf_op jit(solution)/shard_map/convert_element_type | solution.py:91
  112.5 3.6 copy.319
  116.9 4.9 copy.320
  121.8 14.9 %all-to-all-start.1 = ((bf16[512,2,3,449]{3,1,2,0:T(2,128)(2,1)}), bf16[512,2,3,449]{3,1,2,0:T(2,128)(2,1)}, u32[]{:S(2)}, u32[]{:S(2)}) async-start(bf16[512,2,3,449]{3,1,2,0:T(2,128)(2,1)} %copy.320), calls=%async_computation.1 | async-start | bytes 6291456 | tf_op jit(solution)/shard_map/all_to_all | solution.py:99
  139.3 4.9 collective-permute-start
  149.6 117.1 %collective-permute-done = bf16[57,64,56]{1,2,0:T(8,128)(2,1)S(1)} collective-permute-done((bf16[57,64,56]{1,2,0:T(8,128)(2,1)S(1)}, bf16[57,64,56]{1,2,0:T(8,128)(2,1)S(1)}, u32[]{:S(2)}, u32[]{:S(2)}) %collective-permute-start) | collective-permute-done | bytes 408608 | tf_op jit(solution)/shard_map/ppermute | solution.py:108
  275.5 23.7 %all_to_all.75 = f32[64,1,1,56]{3,2,1,0:T(1,128)S(1)} all-to-all(f32[64,1,1,56]{3,2,1,0:T(1,128)S(1)} %constant_dynamic-update-slice_fusion), channel_id=1, replica_groups=mesh['section'=8,'dp'=64] {'dp'}, dimensions={0} | all-to-all | bytes 28672 | tf_op jit(solution)/shard_map/all_to_all | solution.py:127
  300.6 19.9 %all_to_all.76 = bf16[64,2,1792]{2,1,0:T(2,128)(2,1)S(1)} all-to-all(bf16[64,2,1792]{2,1,0:T(2,128)(2,1)S(1)} %reshape.273), channel_id=1, replica_groups=mesh['section'=8,'dp'=64] {'dp'}, dimensions={0} | all-to-all | bytes 917504 | tf_op jit(solution)/shard_map/all_to_all | solution.py:18
  324.7 6.3 %all-to-all-start.5 = ((bf16[64,2,1792]{2,1,0:T(2,128)(2,1)}), bf16[64,2,1792]{2,1,0:T(2,128)(2,1)S(1)}, u32[]{:S(2)}, u32[]{:S(2)}) async-start(bf16[64,2,1792]{2,1,0:T(2,128)(2,1)} %reshape.275), calls=%async_computation.5 | async-start | bytes 917504 | tf_op jit(solution)/shard_map/all_to_all | solution.py:18
  334.5 12.5 %all-to-all-done.5 = bf16[64,2,1792]{2,1,0:T(2,128)(2,1)S(1)} async-done(((bf16[64,2,1792]{2,1,0:T(2,128)(2,1)}), bf16[64,2,1792]{2,1,0:T(2,128)(2,1)S(1)}, u32[]{:S(2)}, u32[]{:S(2)}) %all-to-all-start.5) | async-done | bytes 458784 | tf_op jit(solution)/shard_map/all_to_all | solution.py:18
  350.8 6.6 %all-to-all-start.6 = ((bf16[64,2,1792]{2,1,0:T(2,128)(2,1)}), bf16[64,2,1792]{2,1,0:T(2,128)(2,1)S(1)}, u32[]{:S(2)}, u32[]{:S(2)}) async-start(bf16[64,2,1792]{2,1,0:T(2,128)(2,1)} %reshape.277), calls=%async_computation.6 | async-start | bytes 917504 | tf_op jit(solution)/shard_map/all_to_all | solution.py:18
  360.8 12.4 %all-to-all-done.6 = bf16[64,2,1792]{2,1,0:T(2,128)(2,1)S(1)} async-done(((bf16[64,2,1792]{2,1,0:T(2,128)(2,1)}), bf16[64,2,1792]{2,1,0:T(2,128)(2,1)S(1)}, u32[]{:S(2)}, u32[]{:S(2)}) %all-to-all-start.6) | async-done | bytes 458784 | tf_op jit(solution)/shard_map/all_to_all | solution.py:18
  376.9 6.3 %all-to-all-start.7 = ((bf16[64,2,1792]{2,1,0:T(2,128)(2,1)}), bf16[64,2,1792]{2,1,0:T(2,128)(2,1)S(1)}, u32[]{:S(2)}, u32[]{:S(2)}) async-start(bf16[64,2,1792]{2,1,0:T(2,128)(2,1)} %reshape.279), calls=%async_computation.7 | async-start | bytes 917504 | tf_op jit(solution)/shard_map/all_to_all | solution.py:18
  386.6 12.5 %all-to-all-done.7 = bf16[64,2,1792]{2,1,0:T(2,128)(2,1)S(1)} async-done(((bf16[64,2,1792]{2,1,0:T(2,128)(2,1)}), bf16[64,2,1792]{2,1,0:T(2,128)(2,1)S(1)}, u32[]{:S(2)}, u32[]{:S(2)}) %all-to-all-start.7) | async-done | bytes 458784 | tf_op jit(solution)/shard_map/all_to_all | solution.py:18
  402.9 6.3 %all-to-all-start.8 = ((bf16[64,2,1792]{2,1,0:T(2,128)(2,1)}), bf16[64,2,1792]{2,1,0:T(2,128)(2,1)S(1)}, u32[]{:S(2)}, u32[]{:S(2)}) async-start(bf16[64,2,1792]{2,1,0:T(2,128)(2,1)} %reshape.281), calls=%async_computation.8 | async-start | bytes 917504 | tf_op jit(solution)/shard_map/all_to_all | solution.py:18
  412.6 12.5 %all-to-all-done.8 = bf16[64,2,1792]{2,1,0:T(2,128)(2,1)S(1)} async-done(((bf16[64,2,1792]{2,1,0:T(2,128)(2,1)}), bf16[64,2,1792]{2,1,0:T(2,128)(2,1)S(1)}, u32[]{:S(2)}, u32[]{:S(2)}) %all-to-all-start.8) | async-done | bytes 458784 | tf_op jit(solution)/shard_map/all_to_all | solution.py:18
  428.8 6.6 %all-to-all-start.9 = ((bf16[64,2,1792]{2,1,0:T(2,128)(2,1)}), bf16[64,2,1792]{2,1,0:T(2,128)(2,1)S(1)}, u32[]{:S(2)}, u32[]{:S(2)}) async-start(bf16[64,2,1792]{2,1,0:T(2,128)(2,1)} %reshape.283), calls=%async_computation.9 | async-start | bytes 917504 | tf_op jit(solution)/shard_map/all_to_all | solution.py:18
  438.9 12.4 %all-to-all-done.9 = bf16[64,2,1792]{2,1,0:T(2,128)(2,1)S(1)} async-done(((bf16[64,2,1792]{2,1,0:T(2,128)(2,1)}), bf16[64,2,1792]{2,1,0:T(2,128)(2,1)S(1)}, u32[]{:S(2)}, u32[]{:S(2)}) %all-to-all-start.9) | async-done | bytes 458784 | tf_op jit(solution)/shard_map/all_to_all | solution.py:18
  455.0 6.3 %all-to-all-start.10 = ((bf16[64,2,1792]{2,1,0:T(2,128)(2,1)}), bf16[64,2,1792]{2,1,0:T(2,128)(2,1)S(1)}, u32[]{:S(2)}, u32[]{:S(2)}) async-start(bf16[64,2,1792]{2,1,0:T(2,128)(2,1)} %reshape.285), calls=%async_computation.10 | async-start | bytes 917504 | tf_op jit(solution)/shard_map/all_to_all | solution.py:18
  464.7 12.5 %all-to-all-done.10 = bf16[64,2,1792]{2,1,0:T(2,128)(2,1)S(1)} async-done(((bf16[64,2,1792]{2,1,0:T(2,128)(2,1)}), bf16[64,2,1792]{2,1,0:T(2,128)(2,1)S(1)}, u32[]{:S(2)}, u32[]{:S(2)}) %all-to-all-start.10) | async-done | bytes 458784 | tf_op jit(solution)/shard_map/all_to_all | solution.py:18
  480.3 6.3 %all-to-all-start.11 = ((bf16[64,2,1792]{2,1,0:T(2,128)(2,1)}), bf16[64,2,1792]{2,1,0:T(2,128)(2,1)S(1)}, u32[]{:S(2)}, u32[]{:S(2)}) async-start(bf16[64,2,1792]{2,1,0:T(2,128)(2,1)} %reshape.287), calls=%async_computation.11 | async-start | bytes 917504 | tf_op jit(solution)/shard_map/all_to_all | solution.py:18
  486.6 8.7 %copy.322 = bf16[512,2,3,449]{0,3,2,1:T(8,128)(2,1)} copy(bf16[512,2,3,449]{3,1,2,0:T(2,128)(2,1)} %all-to-all-done.1) | data formatting | bytes 5517312 | tf_op jit(solution)/shard_map/optimization_barrier | solution.py:112
  498.9 3.6 all-to-all-done.11
  503.6 37.0 %all-to-all-start.2 = ((bf16[8,128,448]{1,2,0:T(8,128)(2,1)}), bf16[8,128,448]{1,2,0:T(8,128)(2,1)S(1)}, u32[]{:S(2)}, u32[]{:S(2)}) async-start(bf16[8,128,448]{1,2,0:T(8,128)(2,1)} %broadcast_in_dim.137), calls=%async_computation.2 | async-start | bytes 1835008 | tf_op jit(solution)/shard_map/all_to_all | solution.py:24
  554.3 13.6 %collective-permute-done.13 = f32[2,64,56]{1,2,0:T(8,128)S(1)} collective-permute-done((f32[2,64,56]{1,2,0:T(8,128)S(1)}, f32[2,64,56]{1,2,0:T(8,128)S(1)}, u32[]{:S(2)}, u32[]{:S(2)}) %collective-permute-start.13) | collective-permute-done | bytes 28704 | tf_op jit(solution)/shard_map/ppermute | solution.py:148
  570.2 10.1 %all-to-all-start.12 = ((bf16[64,2,1792]{2,1,0:T(2,128)(2,1)}), bf16[64,2,1792]{2,1,0:T(2,128)(2,1)S(1)}, u32[]{:S(2)}, u32[]{:S(2)}) async-start(bf16[64,2,1792]{2,1,0:T(2,128)(2,1)} %reshape.289), calls=%async_computation.12 | async-start | bytes 917504 | tf_op jit(solution)/shard_map/all_to_all | solution.py:18
  585.0 11.2 %all-to-all-done.12 = bf16[64,2,1792]{2,1,0:T(2,128)(2,1)S(1)} async-done(((bf16[64,2,1792]{2,1,0:T(2,128)(2,1)}), bf16[64,2,1792]{2,1,0:T(2,128)(2,1)S(1)}, u32[]{:S(2)}, u32[]{:S(2)}) %all-to-all-start.12) | async-done | bytes 458784 | tf_op jit(solution)/shard_map/all_to_all | solution.py:18
  (237 shorter events, 105.9 us)
Async XLA Ops:
  0.6 99.6 %copy-start = (bf16[128,3584]{1,0:T(8,128)(2,1)S(1)}, bf16[128,3584]{1,0:T(8,128)(2,1)}, u32[]{:S(2)}) copy-start(bf16[128,3584]{1,0:T(8,128)(2,1)} %param.8) | copy-start | bytes 2752516
  8.1 80.2 %all-to-all-start = ((bf16[2,192,3584]{2,0,1:T(2,128)(2,1)}), bf16[2,192,3584]{2,0,1:T(2,128)(2,1)}, u32[]{:S(2)}, u32[]{:S(2)}) async-start(bf16[2,192,3584]{2,0,1:T(2,128)(2,1)} %copy.315), calls=%async_computation | async-start | bytes 5505024 | tf_op jit(solution)/shard_map/all_to_all | solution.py:50
  121.8 152.9 %all-to-all-start.1 = ((bf16[512,2,3,449]{3,1,2,0:T(2,128)(2,1)}), bf16[512,2,3,449]{3,1,2,0:T(2,128)(2,1)}, u32[]{:S(2)}, u32[]{:S(2)}) async-start(bf16[512,2,3,449]{3,1,2,0:T(2,128)(2,1)} %copy.320), calls=%async_computation.1 | async-start | bytes 6291456 | tf_op jit(solution)/shard_map/all_to_all | solution.py:99
  139.3 127.4 %collective-permute-start = (bf16[57,64,56]{1,2,0:T(8,128)(2,1)S(1)}, bf16[57,64,56]{1,2,0:T(8,128)(2,1)S(1)}, u32[]{:S(2)}, u32[]{:S(2)}) collective-permute-start(bf16[57,64,56]{1,2,0:T(8,128)(2,1)S(1)} %pad_maximum_fusion.1), channel_id=1, source_target_pairs={{0,448},{1,449},{2,450},{3,451},{4,452},{5,453},{6,454},{7,455},{8... | collective-permute-start | bytes 1225736 | tf_op jit(solution)/shard_map/ppermute | solution.py:108
  144.2 124.1 %collective-permute-start.1 = (bf16[57,64,56]{1,2,0:T(8,128)(2,1)S(1)}, bf16[57,64,56]{1,2,0:T(8,128)(2,1)S(1)}, u32[]{:S(2)}, u32[]{:S(2)}) collective-permute-start(bf16[57,64,56]{1,2,0:T(8,128)(2,1)S(1)} %pad_maximum_fusion.1), channel_id=1, source_target_pairs={{64,448},{65,449},{66,450},{67,451},{68,452},{69,453},{70,454},{71... | collective-permute-start | bytes 1225736 | tf_op jit(solution)/shard_map/ppermute | solution.py:108
  144.9 129.7 %collective-permute-start.2 = (bf16[57,64,56]{1,2,0:T(8,128)(2,1)S(1)}, bf16[57,64,56]{1,2,0:T(8,128)(2,1)}, u32[]{:S(2)}, u32[]{:S(2)}) collective-permute-start(bf16[57,64,56]{1,2,0:T(8,128)(2,1)S(1)} %pad_maximum_fusion.1), channel_id=1, source_target_pairs={{128,448},{129,449},{130,450},{131,451},{132,452},{133,453},{134,4... | collective-permute-start | bytes 1225736 | tf_op jit(solution)/shard_map/ppermute | solution.py:108
  146.5 128.1 %collective-permute-start.3 = (bf16[57,64,56]{1,2,0:T(8,128)(2,1)S(1)}, bf16[57,64,56]{1,2,0:T(8,128)(2,1)}, u32[]{:S(2)}, u32[]{:S(2)}) collective-permute-start(bf16[57,64,56]{1,2,0:T(8,128)(2,1)S(1)} %pad_maximum_fusion.1), channel_id=1, source_target_pairs={{192,448},{193,449},{194,450},{195,451},{196,452},{197,453},{198,4... | collective-permute-start | bytes 1225736 | tf_op jit(solution)/shard_map/ppermute | solution.py:108
  148.0 126.6 %collective-permute-start.4 = (bf16[57,64,56]{1,2,0:T(8,128)(2,1)S(1)}, bf16[57,64,56]{1,2,0:T(8,128)(2,1)}, u32[]{:S(2)}, u32[]{:S(2)}) collective-permute-start(bf16[57,64,56]{1,2,0:T(8,128)(2,1)S(1)} %pad_maximum_fusion.1), channel_id=1, source_target_pairs={{256,448},{257,449},{258,450},{259,451},{260,452},{261,453},{262,4... | collective-permute-start | bytes 1225736 | tf_op jit(solution)/shard_map/ppermute | solution.py:108
  266.7 211.0 %copy-start.2 = (bf16[57,64,56]{1,2,0:T(8,128)(2,1)}, bf16[57,64,56]{1,2,0:T(8,128)(2,1)S(1)}, u32[]{:S(2)}) copy-start(bf16[57,64,56]{1,2,0:T(8,128)(2,1)S(1)} %collective-permute-done) | copy-start | bytes 1225732
  266.7 7.9 %collective-permute-start.5 = (bf16[57,64,56]{1,2,0:T(8,128)(2,1)S(1)}, bf16[57,64,56]{1,2,0:T(8,128)(2,1)}, u32[]{:S(2)}, u32[]{:S(2)}) collective-permute-start(bf16[57,64,56]{1,2,0:T(8,128)(2,1)S(1)} %pad_maximum_fusion.1), channel_id=1, source_target_pairs={{320,448},{321,449},{322,450},{323,451},{324,452},{325,453},{326,4... | collective-permute-start | bytes 1225736 | tf_op jit(solution)/shard_map/ppermute | solution.py:108
  269.2 5.5 collective-permute-start.6
  324.7 22.3 %all-to-all-start.5 = ((bf16[64,2,1792]{2,1,0:T(2,128)(2,1)}), bf16[64,2,1792]{2,1,0:T(2,128)(2,1)S(1)}, u32[]{:S(2)}, u32[]{:S(2)}) async-start(bf16[64,2,1792]{2,1,0:T(2,128)(2,1)} %reshape.275), calls=%async_computation.5 | async-start | bytes 917504 | tf_op jit(solution)/shard_map/all_to_all | solution.py:18
  350.8 22.4 %all-to-all-start.6 = ((bf16[64,2,1792]{2,1,0:T(2,128)(2,1)}), bf16[64,2,1792]{2,1,0:T(2,128)(2,1)S(1)}, u32[]{:S(2)}, u32[]{:S(2)}) async-start(bf16[64,2,1792]{2,1,0:T(2,128)(2,1)} %reshape.277), calls=%async_computation.6 | async-start | bytes 917504 | tf_op jit(solution)/shard_map/all_to_all | solution.py:18
  376.9 22.2 %all-to-all-start.7 = ((bf16[64,2,1792]{2,1,0:T(2,128)(2,1)}), bf16[64,2,1792]{2,1,0:T(2,128)(2,1)S(1)}, u32[]{:S(2)}, u32[]{:S(2)}) async-start(bf16[64,2,1792]{2,1,0:T(2,128)(2,1)} %reshape.279), calls=%async_computation.7 | async-start | bytes 917504 | tf_op jit(solution)/shard_map/all_to_all | solution.py:18
  402.9 22.2 %all-to-all-start.8 = ((bf16[64,2,1792]{2,1,0:T(2,128)(2,1)}), bf16[64,2,1792]{2,1,0:T(2,128)(2,1)S(1)}, u32[]{:S(2)}, u32[]{:S(2)}) async-start(bf16[64,2,1792]{2,1,0:T(2,128)(2,1)} %reshape.281), calls=%async_computation.8 | async-start | bytes 917504 | tf_op jit(solution)/shard_map/all_to_all | solution.py:18
  428.8 22.4 %all-to-all-start.9 = ((bf16[64,2,1792]{2,1,0:T(2,128)(2,1)}), bf16[64,2,1792]{2,1,0:T(2,128)(2,1)S(1)}, u32[]{:S(2)}, u32[]{:S(2)}) async-start(bf16[64,2,1792]{2,1,0:T(2,128)(2,1)} %reshape.283), calls=%async_computation.9 | async-start | bytes 917504 | tf_op jit(solution)/shard_map/all_to_all | solution.py:18
  455.0 22.2 %all-to-all-start.10 = ((bf16[64,2,1792]{2,1,0:T(2,128)(2,1)}), bf16[64,2,1792]{2,1,0:T(2,128)(2,1)S(1)}, u32[]{:S(2)}, u32[]{:S(2)}) async-start(bf16[64,2,1792]{2,1,0:T(2,128)(2,1)} %reshape.285), calls=%async_computation.10 | async-start | bytes 917504 | tf_op jit(solution)/shard_map/all_to_all | solution.py:18
  480.3 22.2 %all-to-all-start.11 = ((bf16[64,2,1792]{2,1,0:T(2,128)(2,1)}), bf16[64,2,1792]{2,1,0:T(2,128)(2,1)S(1)}, u32[]{:S(2)}, u32[]{:S(2)}) async-start(bf16[64,2,1792]{2,1,0:T(2,128)(2,1)} %reshape.287), calls=%async_computation.11 | async-start | bytes 917504 | tf_op jit(solution)/shard_map/all_to_all | solution.py:18
  496.0 44.6 %copy-start.3 = (bf16[57,64,56]{1,2,0:T(8,128)(2,1)S(1)}, bf16[57,64,56]{1,2,0:T(8,128)(2,1)}, u32[]{:S(2)}) copy-start(bf16[57,64,56]{1,2,0:T(8,128)(2,1)} %copy-done.2) | copy-start | bytes 1225732
  503.6 45.7 %copy-start.9 = (f32[64,56]{0,1:T(8,128)S(1)}, f32[64,56]{0,1:T(8,128)}, u32[]{:S(2)}) copy-start(f32[64,56]{0,1:T(8,128)} %copy-done.8) | copy-start | bytes 43012
  503.6 45.7 %copy-start.17 = (f32[1,64,56]{1,2,0:T(8,128)S(1)}, f32[1,64,56]{1,2,0:T(8,128)}, u32[]{:S(2)}) copy-start(f32[1,64,56]{1,2,0:T(8,128)} %get-tuple-element.30) | copy-start | bytes 43012
  503.6 47.0 %copy-start.10 = (f32[64,56]{0,1:T(8,128)S(1)}, f32[64,56]{0,1:T(8,128)}, u32[]{:S(2)}) copy-start(f32[64,56]{0,1:T(8,128)} %get-tuple-element.46) | copy-start | bytes 43012
  503.6 47.0 %copy-start.18 = (f32[1,64,56]{1,2,0:T(8,128)S(1)}, f32[1,64,56]{1,2,0:T(8,128)}, u32[]{:S(2)}) copy-start(f32[1,64,56]{1,2,0:T(8,128)} %get-tuple-element.32) | copy-start | bytes 43012
  503.6 66.6 %all-to-all-start.2 = ((bf16[8,128,448]{1,2,0:T(8,128)(2,1)}), bf16[8,128,448]{1,2,0:T(8,128)(2,1)S(1)}, u32[]{:S(2)}, u32[]{:S(2)}) async-start(bf16[8,128,448]{1,2,0:T(8,128)(2,1)} %broadcast_in_dim.137), calls=%async_computation.2 | async-start | bytes 1835008 | tf_op jit(solution)/shard_map/all_to_all | solution.py:24
  543.5 8.7 %collective-permute-start.7 = (f32[2,64,56]{1,2,0:T(8,128)}, f32[2,64,56]{1,2,0:T(8,128)}, u32[]{:S(2)}, u32[]{:S(2)}) collective-permute-start(f32[2,64,56]{1,2,0:T(8,128)} %pad_maximum_fusion.2), channel_id=1, source_target_pairs={{448,384},{449,385},{450,386},{451,387},{452,388},{453,389},{454,3... | collective-permute-start | bytes 86024 | tf_op jit(solution)/shard_map/ppermute | solution.py:148
  545.4 7.5 %collective-permute-start.8 = (f32[2,64,56]{1,2,0:T(8,128)}, f32[2,64,56]{1,2,0:T(8,128)}, u32[]{:S(2)}, u32[]{:S(2)}) collective-permute-start(f32[2,64,56]{1,2,0:T(8,128)} %pad_maximum_fusion.3), channel_id=1, source_target_pairs={{448,320},{449,321},{450,322},{451,323},{452,324},{453,325},{454,3... | collective-permute-start | bytes 86024 | tf_op jit(solution)/shard_map/ppermute | solution.py:148
  546.7 7.5 %collective-permute-start.9 = (f32[2,64,56]{1,2,0:T(8,128)S(1)}, f32[2,64,56]{1,2,0:T(8,128)}, u32[]{:S(2)}, u32[]{:S(2)}) collective-permute-start(f32[2,64,56]{1,2,0:T(8,128)S(1)} %pad_maximum_fusion.4), channel_id=1, source_target_pairs={{448,256},{449,257},{450,258},{451,259},{452,260},{453,261},{454,2... | collective-permute-start | bytes 86024 | tf_op jit(solution)/shard_map/ppermute | solution.py:148
  548.0 6.3 %collective-permute-start.10 = (f32[2,64,56]{1,2,0:T(8,128)S(1)}, f32[2,64,56]{1,2,0:T(8,128)}, u32[]{:S(2)}, u32[]{:S(2)}) collective-permute-start(f32[2,64,56]{1,2,0:T(8,128)S(1)} %pad_maximum_fusion.5), channel_id=1, source_target_pairs={{448,192},{449,193},{450,194},{451,195},{452,196},{453,197},{454,1... | collective-permute-start | bytes 86024 | tf_op jit(solution)/shard_map/ppermute | solution.py:148
  549.3 5.0 collective-permute-start.11
  552.3 2.0 collective-permute-start.12
  552.9 14.9 %collective-permute-start.13 = (f32[2,64,56]{1,2,0:T(8,128)S(1)}, f32[2,64,56]{1,2,0:T(8,128)S(1)}, u32[]{:S(2)}, u32[]{:S(2)}) collective-permute-start(f32[2,64,56]{1,2,0:T(8,128)S(1)} %pad_maximum_fusion.8), channel_id=1, source_target_pairs={{448,0},{449,1},{450,2},{451,3},{452,4},{453,5},{454,6},{455,7},{4... | collective-permute-start | bytes 86024 | tf_op jit(solution)/shard_map/ppermute | solution.py:148
  570.2 26.1 %all-to-all-start.12 = ((bf16[64,2,1792]{2,1,0:T(2,128)(2,1)}), bf16[64,2,1792]{2,1,0:T(2,128)(2,1)S(1)}, u32[]{:S(2)}, u32[]{:S(2)}) async-start(bf16[64,2,1792]{2,1,0:T(2,128)(2,1)} %reshape.289), calls=%async_computation.12 | async-start | bytes 917504 | tf_op jit(solution)/shard_map/all_to_all | solution.py:18
  (20 other events, 422.6 us)
